TPU v7x, 32 devices: a whole 2x2x4 slice. The times are simulated.
32 devices in a mesh: rows: 4 (over x, core), dp: 8 (over z, y).
Axes of the slice: x: 2, y: 2, z: 4, core: 2. Of those that a mesh axis runs over, the one named last changes fastest.
Arguments:
- latents: bfloat16 [8, 8, 128, 640], P('dp', 'rows'), may hold values from -160 to 160
- timesteps: int32 [8], P('dp'), may hold values from 0 to 999
- gn_gain: float32 [640], replicated, may hold values from 0.1 to 1.9
- gn_bias: float32 [640], replicated, may hold values from -3 to 3
- conv_weight: bfloat16 [3, 3, 640, 640], replicated, may hold values from -0.078125 to 0.078125
- conv_bias: float32 [640], replicated, may hold values from -3 to 3
- temb_weight: bfloat16 [1280, 640], replicated, may hold values from -0.25 to 0.25
- cotangent: bfloat16 [8, 8, 128, 640], P('dp', 'rows'), may hold values from -6 to 6
Outputs:
- features_out: bfloat16 [8, 8, 128, 640], P('dp', 'rows')
- input_grad: bfloat16 [8, 8, 128, 640], P('dp', 'rows')
- norm_grads: float32 [3, 640], replicated
All inputs are finite; a program needn't handle non-finite values.
Results may differ from a plain program's by a relative error of at most 0.0044.
Values may be sent and summed in bfloat16 or wider, within the bound.
No kernel may reach another device: no remote copies, remote signals or barrier semaphores. Data moves between devices by JAX's collectives and lax.ppermute only.
A program may use at most 64 MiB of HBM per device.

v0:
```python
import math
import jax
import jax.numpy as jnp
from jax import lax
from jax.sharding import PartitionSpec as P

CH_GROUP = 40
NORM_EPS = 1e-05


def padded_2(cells, sides, width):
    for axis, dim in sides:
        count = lax.axis_size(axis)
        ends = count - 1
        head = lax.slice_in_dim(cells, 0, width, axis=dim)
        tail = lax.slice_in_dim(cells, cells.shape[dim] - width, cells.shape[dim], axis=dim)
        cells = jnp.concatenate(
            [
                lax.ppermute(tail, axis, [(i, (i + 1) % count) for i in range(ends)]),
                cells,
                lax.ppermute(head, axis, [((i + 1) % count, i) for i in range(ends)]),
            ],
            axis=dim,
        )
    return cells


def sinusoid(steps, embed_dim):
    half_dim = embed_dim // 2
    frequencies = jnp.exp(-math.log(10000.0) * jnp.arange(half_dim).astype(jnp.float32) / half_dim)
    angles = steps.astype(jnp.float32)[:, None] * frequencies[None, :]
    return jnp.concatenate([jnp.cos(angles), jnp.sin(angles)], axis=1)


def with_rim(field):
    return padded_2(field, (("rows", 1),), 1)


def conv_taps(extended, weight, slab_rows, col_count, backward):
    padded = jnp.pad(extended, ((0, 0), (0, 0), (1, 1), (0, 0)))
    images = padded.shape[0]
    channels = padded.shape[3]
    total = None
    for tap_row in range(3):
        for tap_col in range(3):
            if backward:
                row_start, col_start = (2 - tap_row, 2 - tap_col)
            else:
                row_start, col_start = (tap_row, tap_col)
            window = padded[
                :, row_start : row_start + slab_rows, col_start : col_start + col_count
            ].reshape(-1, channels)
            if backward:
                tap_term = lax.dot_general(
                    window,
                    weight[tap_row, tap_col],
                    (((1,), (1,)), ((), ())),
                    preferred_element_type=jnp.float32,
                )
            else:
                tap_term = jnp.dot(
                    window, weight[tap_row, tap_col], preferred_element_type=jnp.float32
                )
            total = tap_term if total is None else total + tap_term
    return total.reshape(images, slab_rows, col_count, -1)


def per_device(
    latents, timesteps, gn_gain, gn_bias, conv_weight, conv_bias, temb_weight, cotangent
):
    images, slab_rows, col_count, channels = latents.shape
    groups = channels // CH_GROUP
    row_devices = lax.axis_size("rows")
    group_cells = slab_rows * row_devices * col_count * CH_GROUP
    grouped = latents.astype(jnp.float32).reshape(images, slab_rows, col_count, groups, CH_GROUP)
    totals, squares = lax.psum(
        (jnp.sum(grouped, axis=(1, 2, 4)), jnp.sum(grouped * grouped, axis=(1, 2, 4))), "rows"
    )
    group_mean = totals / group_cells
    inv_std = lax.rsqrt(squares / group_cells - group_mean * group_mean + NORM_EPS)
    shaped = latents.astype(jnp.float32).reshape(images, -1, col_count, groups, CH_GROUP)
    norm_groups = (shaped - group_mean[:, None, None, :, None]) * inv_std[:, None, None, :, None]
    normalized = norm_groups.reshape(images, -1, col_count, channels)
    norm_groups, normalized, pre_act = (norm_groups, normalized, normalized * gn_gain + gn_bias)
    hidden = jax.nn.silu(pre_act).astype(jnp.bfloat16)
    grad_rim = None
    extended = with_rim(hidden)
    temb_features = jax.nn.silu(sinusoid(timesteps, temb_weight.shape[0])).astype(jnp.bfloat16)
    time_shift = jnp.dot(temb_features, temb_weight, preferred_element_type=jnp.float32)
    features = conv_taps(extended, conv_weight, slab_rows, col_count, False)
    features_out = (features + conv_bias + time_shift[:, None, None, :]).astype(jnp.bfloat16)
    grad_rim = with_rim(cotangent)
    hidden_grad = conv_taps(grad_rim, conv_weight, slab_rows, col_count, True)
    sigmoid_act = jax.nn.sigmoid(pre_act)
    act_grad = hidden_grad * sigmoid_act * (1.0 + pre_act * (1.0 - sigmoid_act))
    hat_groups = (act_grad * gn_gain).reshape(images, slab_rows, col_count, groups, CH_GROUP)
    chan_weighted = jnp.sum(act_grad * normalized, axis=(1, 2))
    chan_plain = jnp.sum(act_grad, axis=(1, 2))
    chan_output = jnp.sum(cotangent.astype(jnp.float32), axis=(1, 2))
    row_weighted, row_plain, row_output = lax.psum((chan_weighted, chan_plain, chan_output), "rows")
    first_sum = jnp.sum((row_plain * gn_gain).reshape(images, groups, CH_GROUP), axis=2)
    second_sum = jnp.sum((row_weighted * gn_gain).reshape(images, groups, CH_GROUP), axis=2)
    image_terms = jnp.stack(
        [jnp.sum(row_weighted, axis=0), jnp.sum(row_plain, axis=0), jnp.sum(row_output, axis=0)]
    )
    param_sums = lax.psum(image_terms, "dp")
    first_mean = first_sum / group_cells
    second_mean = second_sum / group_cells
    expand = (slice(None), None, None, slice(None), None)
    input_grad = inv_std[expand] * (
        hat_groups - first_mean[expand] - norm_groups * second_mean[expand]
    )
    input_grad = input_grad.reshape(images, slab_rows, col_count, channels).astype(jnp.bfloat16)
    grad_scale = 1.0 / math.sqrt(images * lax.axis_size("dp") * slab_rows * row_devices * col_count)
    return (features_out, input_grad, param_sums * grad_scale)


def solution(mesh):
    placed = (
        P("dp", "rows", None, None),
        P("dp"),
        P(),
        P(),
        P(),
        P(),
        P(),
        P("dp", "rows", None, None),
    )
    return jax.shard_map(
        per_device,
        mesh=mesh,
        in_specs=placed,
        out_specs=(P("dp", "rows", None, None), P("dp", "rows", None, None), P()),
        check_vma=False,
    )
```

profile of v0, /device:TPU:1, one launch (start us, length us, event | category | flops | bytes accessed | tf_op | source)
XLA Modules:
  0.0 90.6 jit_solution(9384634397204570961)
XLA Ops:
  0.7 1.2 %fusion.69 = (bf16[1,1,128,640]{3,2,1,0:T(8,128)(2,1)S(1)}, bf16[1,1,128,640]{3,2,1,0:T(8,128)(2,1)S(1)}) fusion(bf16[1,2,128,640]{3,2,1,0:T(8,128)(2,1)} %param.15), kind=kLoop, calls=%fused_computation.109 | loop fusion | bytes 655360 | tf_op jit(solution)/shard_map/slice | solution.py:16
  1.8 4.5 %collective-permute-start.2 = (bf16[1,1,128,640]{3,2,1,0:T(8,128)(2,1)S(1)}, bf16[1,1,128,640]{3,2,1,0:T(8,128)(2,1)S(1)}, u32[]{:S(2)}, u32[]{:S(2)}) collective-permute-start(bf16[1,1,128,640]{3,2,1,0:T(8,128)(2,1)S(1)} %get-tuple-element.30), channel_id=1, source_target_pairs={{0,8},{8,16},{16,24},{1,9},{9,17},{17,25},{2,10},{10,18},{18,26},{... | collective-permute-start | bytes 491528 | tf_op jit(solution)/shard_map/ppermute | solution.py:19
  6.3 1.9 %collective-permute-start.3 = (bf16[1,1,128,640]{3,2,1,0:T(8,128)(2,1)S(1)}, bf16[1,1,128,640]{3,2,1,0:T(8,128)(2,1)S(1)}, u32[]{:S(2)}, u32[]{:S(2)}) collective-permute-start(bf16[1,1,128,640]{3,2,1,0:T(8,128)(2,1)S(1)} %get-tuple-element.31), channel_id=1, source_target_pairs={{8,0},{16,8},{24,16},{9,1},{17,9},{25,17},{10,2},{18,10},{26,18},{... | collective-permute-start | bytes 491528 | tf_op jit(solution)/shard_map/ppermute | solution.py:21
  8.3 1.0 %convert_reduce_fusion.1 = f32[640]{0:T(1024)S(1)} fusion(bf16[1,2,128,640]{3,2,1,0:T(8,128)(2,1)} %param.15), kind=kLoop, calls=%fused_computation.87 | loop fusion | flops 327040 | bytes 330240 | tf_op jit(solution)/shard_map/reduce_sum | solution.py:99
  9.3 1.1 %convert_reduce_fusion = (f32[640]{0:T(1024)S(1)}, f32[640]{0:T(1024)S(1)}) fusion(bf16[1,2,128,640]{3,2,1,0:T(8,128)(2,1)} %param.8), kind=kLoop, calls=%fused_computation.22 | loop fusion | flops 654080 | bytes 332800 | tf_op jit(solution)/shard_map/reduce_sum | solution.py:77
  10.8 5.5 %all-reduce.3 = (f32[1,16]{1,0:T(1,128)S(1)}, f32[1,16]{1,0:T(1,128)S(1)}) all-reduce(f32[1,16]{1,0:T(1,128)S(1)} %bitcast.115, f32[1,16]{1,0:T(1,128)S(1)} %bitcast.114), channel_id=1, replica_groups=mesh['rows'=4,'dp'=8] {'rows'}, use_global_device_ids=true, to_apply=%region_5.6 | all-reduce | flops 32 | bytes 256 | tf_op jit(solution)/shard_map/psum | solution.py:76
  17.9 1.5 %select_maximum_fusion = bf16[1,4,130,640]{3,2,1,0:T(8,128)(2,1)S(1)} fusion(bf16[1,1,128,640]{3,2,1,0:T(8,128)(2,1)S(1)} %collective-permute-done.3, bf16[1,2,128,640]{3,2,1,0:T(8,128)(2,1)} %param.15, bf16[1,1,128,640]{3,2,1,0:T(8,128)(2,1)S(1)} %collective-permute-done.2), kind=kLoop, calls=%fused_computation.63 | loop fusion | flops 3993600 | bytes 1320960 | tf_op jit(solution)/shard_map/concatenate | solution.py:17
  19.6 1.6 %fusion.21 = f32[256,640]{1,0:T(8,128)S(1)} fusion(bf16[256,640]{1,0:T(8,128)(2,1)S(1)} %bitcast.112, bf16[3,3,640,640]{3,2,1,0:T(8,128)(2,1)} %param.12), kind=kOutput, calls=%fused_computation.41 | convolution fusion | flops 209715200 | bytes 1802240 | tf_op jit(solution)/shard_map/dot_general | solution.py:54
  21.3 0.5 fusion.3
  21.8 0.5 convolution_add_fusion.6
  22.3 0.5 convolution_add_fusion.5
  22.8 0.5 convolution_add_fusion.4
  23.3 0.5 convolution_add_fusion.3
  23.8 0.5 convolution_add_fusion.2
  24.2 0.5 convolution_add_fusion.1
  24.7 0.5 fusion.2
  25.7 5.8 %all-reduce.2 = (f32[1,640]{1,0:T(1,128)S(1)}, f32[1,640]{1,0:T(1,128)S(1)}, f32[1,640]{1,0:T(1,128)S(1)}) all-reduce(f32[1,640]{1,0:T(1,128)S(1)} %reduce_sum.108, f32[1,640]{1,0:T(1,128)S(1)} %reduce_sum.111, f32[1,640]{1,0:T(1,128)S(1)} %reduce_sum.114), channel_id=1, replica_groups=mesh['rows'=4,'dp'=8] {'rows'}, use_global_device_ids=true, to_apply=%region_7.8 | all-reduce | flops 1920 | bytes 15360 | tf_op jit(solution)/shard_map/psum | solution.py:100
  31.5 30.2 %psum.47 = f32[3,640]{1,0:T(4,128)S(1)} all-reduce(f32[3,640]{1,0:T(4,128)S(1)} %pad_maximum_fusion.4), channel_id=1, replica_groups=mesh['rows'=4,'dp'=8] {'dp'}, use_global_device_ids=true, to_apply=%region_14.15 | all-reduce | flops 1920 | bytes 15360 | tf_op jit(solution)/shard_map/psum | solution.py:106
  62.6 11.1 %collective-permute-start = (bf16[1,1,128,640]{3,2,1,0:T(8,128)(2,1)S(1)}, bf16[1,1,128,640]{3,2,1,0:T(8,128)(2,1)S(1)}, u32[]{:S(2)}, u32[]{:S(2)}) collective-permute-start(bf16[1,1,128,640]{3,2,1,0:T(8,128)(2,1)S(1)} %get-tuple-element.34), channel_id=1, source_target_pairs={{0,8},{8,16},{16,24},{1,9},{9,17},{17,25},{2,10},{10,18},{18,26},{... | collective-permute-start | bytes 491528 | tf_op jit(solution)/shard_map/ppermute | solution.py:19
  73.7 1.9 %collective-permute-start.1 = (bf16[1,1,128,640]{3,2,1,0:T(8,128)(2,1)S(1)}, bf16[1,1,128,640]{3,2,1,0:T(8,128)(2,1)S(1)}, u32[]{:S(2)}, u32[]{:S(2)}) collective-permute-start(bf16[1,1,128,640]{3,2,1,0:T(8,128)(2,1)S(1)} %get-tuple-element.35), channel_id=1, source_target_pairs={{8,0},{16,8},{24,16},{9,1},{17,9},{25,17},{10,2},{18,10},{26,18},{... | collective-permute-start | bytes 491528 | tf_op jit(solution)/shard_map/ppermute | solution.py:21
  75.6 0.9 %fusion.61 = bf16[1,2,128,640]{3,2,1,0:T(8,128)(2,1)} fusion(bf16[1,2,128,640]{3,2,1,0:T(8,128)(2,1)S(1)} %copy-done.3, f32[1,2,128,640]{3,2,1,0:T(8,128)S(1)} %get-tuple-element.14, f32[640]{0:T(1024)S(1)} %mul.180, f32[640]{0:T(1024)S(1)} %sub.67, f32[640]{0:T(1024)S(1)} %copy-done.4, f32[640]{0:T(1024)S(1)} %mul.162, f32[640]{0:T(1024)S(1)} %sub.61), kind=kLoop, calls=%fused_computation.85 | loop fusion | flops 1474560 | bytes 1323520 | tf_op jit(solution)/shard_map/convert_element_type | solution.py:113
  76.5 0.6 broadcast_multiply_fusion
  77.1 3.2 %collective-permute-done.1 = bf16[1,1,128,640]{3,2,1,0:T(8,128)(2,1)S(1)} collective-permute-done((bf16[1,1,128,640]{3,2,1,0:T(8,128)(2,1)S(1)}, bf16[1,1,128,640]{3,2,1,0:T(8,128)(2,1)S(1)}, u32[]{:S(2)}, u32[]{:S(2)}) %collective-permute-start.1) | collective-permute-done | bytes 163872 | tf_op jit(solution)/shard_map/ppermute | solution.py:21
  80.8 1.6 %fusion.23 = f32[256,640]{1,0:T(8,128)S(1)} fusion(bf16[256,640]{1,0:T(8,128)(2,1)S(1)} %bitcast.113, bf16[3,3,640,640]{3,2,1,0:T(8,128)(2,1)} %param.12), kind=kOutput, calls=%fused_computation.43 | convolution fusion | flops 209715200 | bytes 1802240 | tf_op jit(solution)/shard_map/dot_general | solution.py:61
  82.4 1.8 %fusion.5 = f32[256,640]{1,0:T(8,128)S(1)} fusion(bf16[256,640]{1,0:T(8,128)(2,1)S(1)} %bitcast.111, bf16[3,3,640,640]{3,2,1,0:T(8,128)(2,1)} %param.12), kind=kOutput, calls=%fused_computation.25 | convolution fusion | flops 209715200 | bytes 1802240 | tf_op jit(solution)/shard_map/dot_general | solution.py:61
  84.2 1.6 %convolution_add_fusion.13 = f32[256,640]{1,0:T(8,128)S(1)} fusion(f32[256,640]{1,0:T(8,128)S(1)} %fusion.23, bf16[256,640]{1,0:T(8,128)(2,1)S(1)} %bitcast.101, bf16[3,3,640,640]{3,2,1,0:T(8,128)(2,1)} %param.12), kind=kOutput, calls=%fused_computation.16 | convolution fusion | flops 209879040 | bytes 2457600 | tf_op jit(solution)/shard_map/dot_general | solution.py:61
  85.9 1.6 %convolution_add_fusion.12 = f32[256,640]{1,0:T(8,128)S(1)} fusion(f32[256,640]{1,0:T(8,128)S(1)} %convolution_add_fusion.13, bf16[256,640]{1,0:T(8,128)(2,1)S(1)} %bitcast.109, bf16[3,3,640,640]{3,2,1,0:T(8,128)(2,1)} %param.12), kind=kOutput, calls=%fused_computation.15 | convolution fusion | flops 209879040 | bytes 2457600 | tf_op jit(solution)/shard_map/dot_general | solution.py:61
  87.5 0.5 convolution_add_fusion.11
  88.0 0.5 convolution_add_fusion.10
  88.9 0.5 convolution_add_fusion.8
  89.4 0.5 fusion.1
  89.8 0.8 add_convert_fusion
  (58 shorter events, 3.7 us)
Async XLA Ops:
  0.6 16.9 %copy-start = (bf16[1280,640]{1,0:T(8,128)(2,1)S(1)}, bf16[1280,640]{1,0:T(8,128)(2,1)}, u32[]{:S(2)}) copy-start(bf16[1280,640]{1,0:T(8,128)(2,1)} %param.14) | copy-start | bytes 4915204
  0.6 21.1 %copy-start.2 = (bf16[1,2,128,640]{3,2,1,0:T(8,128)(2,1)S(1)}, bf16[1,2,128,640]{3,2,1,0:T(8,128)(2,1)}, u32[]{:S(2)}) copy-start(bf16[1,2,128,640]{3,2,1,0:T(8,128)(2,1)} %param.15) | copy-start | bytes 983044
  1.8 16.1 %collective-permute-start.2 = (bf16[1,1,128,640]{3,2,1,0:T(8,128)(2,1)S(1)}, bf16[1,1,128,640]{3,2,1,0:T(8,128)(2,1)S(1)}, u32[]{:S(2)}, u32[]{:S(2)}) collective-permute-start(bf16[1,1,128,640]{3,2,1,0:T(8,128)(2,1)S(1)} %get-tuple-element.30), channel_id=1, source_target_pairs={{0,8},{8,16},{16,24},{1,9},{9,17},{17,25},{2,10},{10,18},{18,26},{... | collective-permute-start | bytes 491528 | tf_op jit(solution)/shard_map/ppermute | solution.py:19
  6.3 11.6 %collective-permute-start.3 = (bf16[1,1,128,640]{3,2,1,0:T(8,128)(2,1)S(1)}, bf16[1,1,128,640]{3,2,1,0:T(8,128)(2,1)S(1)}, u32[]{:S(2)}, u32[]{:S(2)}) collective-permute-start(bf16[1,1,128,640]{3,2,1,0:T(8,128)(2,1)S(1)} %get-tuple-element.31), channel_id=1, source_target_pairs={{8,0},{16,8},{24,16},{9,1},{17,9},{25,17},{10,2},{18,10},{26,18},{... | collective-permute-start | bytes 491528 | tf_op jit(solution)/shard_map/ppermute | solution.py:21
  16.6 4.6 %copy-start.1 = (bf16[3,3,640,640]{3,2,1,0:T(8,128)(2,1)S(1)}, bf16[3,3,640,640]{3,2,1,0:T(8,128)(2,1)}, u32[]{:S(2)}) copy-start(bf16[3,3,640,640]{3,2,1,0:T(8,128)(2,1)} %param.12) | copy-start | bytes 22118404
  22.3 2.9 %copy-start.3 = (bf16[1,2,128,640]{3,2,1,0:T(8,128)(2,1)S(1)}, bf16[1,2,128,640]{3,2,1,0:T(8,128)(2,1)}, u32[]{:S(2)}) copy-start(bf16[1,2,128,640]{3,2,1,0:T(8,128)(2,1)} %param.8) | copy-start | bytes 983044
  22.3 2.9 %copy-start.4 = (f32[640]{0:T(1024)S(1)}, f32[640]{0:T(1024)}, u32[]{:S(2)}) copy-start(f32[640]{0:T(1024)} %param.10) | copy-start | bytes 7684
  22.3 2.9 %copy-start.5 = (f32[640]{0:T(1024)S(1)}, f32[640]{0:T(1024)}, u32[]{:S(2)}) copy-start(f32[640]{0:T(1024)} %param.11) | copy-start | bytes 7684
  62.6 14.6 %collective-permute-start = (bf16[1,1,128,640]{3,2,1,0:T(8,128)(2,1)S(1)}, bf16[1,1,128,640]{3,2,1,0:T(8,128)(2,1)S(1)}, u32[]{:S(2)}, u32[]{:S(2)}) collective-permute-start(bf16[1,1,128,640]{3,2,1,0:T(8,128)(2,1)S(1)} %get-tuple-element.34), channel_id=1, source_target_pairs={{0,8},{8,16},{16,24},{1,9},{9,17},{17,25},{2,10},{10,18},{18,26},{... | collective-permute-start | bytes 491528 | tf_op jit(solution)/shard_map/ppermute | solution.py:19
  73.7 6.6 %collective-permute-start.1 = (bf16[1,1,128,640]{3,2,1,0:T(8,128)(2,1)S(1)}, bf16[1,1,128,640]{3,2,1,0:T(8,128)(2,1)S(1)}, u32[]{:S(2)}, u32[]{:S(2)}) collective-permute-start(bf16[1,1,128,640]{3,2,1,0:T(8,128)(2,1)S(1)} %get-tuple-element.35), channel_id=1, source_target_pairs={{8,0},{16,8},{24,16},{9,1},{17,9},{25,17},{10,2},{18,10},{26,18},{... | collective-permute-start | bytes 491528 | tf_op jit(solution)/shard_map/ppermute | solution.py:21
  77.1 10.4 %slice-start = ((s8[7372800]{0:T(1024)(128)(4,1)}), s8[3178496]{0:T(1024)(128)(4,1)S(1)}, s32[]{:S(2)}) async-start(s8[7372800]{0:T(1024)(128)(4,1)} %bitcast.93), calls=%async_computation | async-start | bytes 6356992
  82.4 5.1 %slice-start.1 = ((s8[7372800]{0:T(1024)(128)(4,1)}), s8[4194304]{0:T(1024)(128)(4,1)S(1)}, s32[]{:S(2)}) async-start(s8[7372800]{0:T(1024)(128)(4,1)} %bitcast.93), calls=%async_computation.1 | async-start | bytes 8388608
  85.8 4.0 %copy-start.6 = (f32[640]{0:T(1024)S(1)}, f32[640]{0:T(1024)}, u32[]{:S(2)}) copy-start(f32[640]{0:T(1024)} %param.13) | copy-start | bytes 7684
where the time goes:
time: 91.1 us; the launch traced here: 90.6 us
  blocking collectives  41.6 us (46%)
  starting transfers between devices  19.4 us (21%)
  matrix products  14.6 us (16%)
  other arithmetic  7.23 us (8%)
  waiting for transfers between devices  3.2 us (4%)
  local copies, waits for them, and re-layouts  2.72 us (3%)
  between operations  1.93 us (2%)
    psum x1, blocking collectives, per_device(): param_sums = lax.psum(image_terms, 'dp')  30.2 us
    ppermute x2, starting transfers between devices, padded_2(): lax.ppermute(tail, axis, [(i, (i + 1) % count) for i in range(ends)])  15.6 us
    dot_general x9, matrix products, conv_taps(): jnp.dot(window, weight[tap_row, tap_col], preferred_element_type=jnp.floa...  8.88 us
    psum x1, blocking collectives, per_device(): lax.psum((chan_weighted, chan_plain, chan_output), 'rows')  5.81 us
    psum x1, blocking collectives, per_device(): lax.psum((jnp.sum(grouped, axis=(1, 2, 4)), jnp.sum(grouped * grouped, ax...  5.51 us
    dot_general x9, matrix products, conv_taps(): lax.dot_general(window, weight[tap_row, tap_col], (((1,), (1,)), ((), ())...  5.35 us
    ppermute x2, starting transfers between devices, padded_2(): lax.ppermute(head, axis, [((i + 1) % count, i) for i in range(ends)])  3.84 us
    ppermute x2, waiting for transfers between devices, padded_2(): lax.ppermute(head, axis, [((i + 1) % count, i) for i in range(ends)])  3.19 us
  transfers between devices with their start and end apart: 4, of which 1 were waited for; matrix products, arithmetic and copies ran while one was open for 5% of the time, Pallas kernels for 0%

commit v1 on v0

--- a/solution.py
+++ b/solution.py
@@ -103,7 +103,7 @@
     image_terms = jnp.stack(
         [jnp.sum(row_weighted, axis=0), jnp.sum(row_plain, axis=0), jnp.sum(row_output, axis=0)]
     )
-    param_sums = lax.psum(image_terms, "dp")
+    param_sums = jnp.sum(lax.all_gather(image_terms, "dp"), axis=0)
     first_mean = first_sum / group_cells
     second_mean = second_sum / group_cells
     expand = (slice(None), None, None, slice(None), None)

time: 91.1 us -> 84.6 us (0.929)
  blocking collectives: 41.6 us -> 36 us
    psum x1 -> x0, blocking collectives: 30.2 us -> none  [per_device(): param_sums = lax.psum(image_terms, 'dp')]
    all_gather x0 -> x1, blocking collectives: none -> 24.7 us  [per_device(): param_sums = jnp.sum(lax.all_gather(image_terms, 'dp'), axis=0)]
    ppermute x2, starting transfers between devices: 15.6 us -> 14.6 us  [padded_2(): lax.ppermute(tail, axis, [(i, (i + 1) % count) for i in range(ends)])]
  transfers between devices with their start and end apart: 4 -> 4, of which waited for: 1 -> 1; matrix products, arithmetic and copies ran while one was open for 5% -> 6% of each run, Pallas kernels for 0% -> 0%
where the time goes in v1:
time: 84.6 us; the launch traced here: 84.1 us
  blocking collectives  36 us (43%)
  starting transfers between devices  18.5 us (22%)
  matrix products  14.6 us (17%)
  other arithmetic  7.25 us (9%)
  waiting for transfers between devices  3.2 us (4%)
  local copies, waits for them, and re-layouts  2.73 us (3%)
  between operations  1.93 us (2%)
    all_gather x1, blocking collectives, per_device(): param_sums = jnp.sum(lax.all_gather(image_terms, 'dp'), axis=0)  24.7 us
    ppermute x2, starting transfers between devices, padded_2(): lax.ppermute(tail, axis, [(i, (i + 1) % count) for i in range(ends)])  14.6 us
    dot_general x9, matrix products, conv_taps(): jnp.dot(window, weight[tap_row, tap_col], preferred_element_type=jnp.floa...  8.88 us
    psum x1, blocking collectives, per_device(): lax.psum((chan_weighted, chan_plain, chan_output), 'rows')  5.81 us
    psum x1, blocking collectives, per_device(): lax.psum((jnp.sum(grouped, axis=(1, 2, 4)), jnp.sum(grouped * grouped, ax...  5.51 us
    dot_general x9, matrix products, conv_taps(): lax.dot_general(window, weight[tap_row, tap_col], (((1,), (1,)), ((), ())...  5.35 us
    ppermute x2, starting transfers between devices, padded_2(): lax.ppermute(head, axis, [((i + 1) % count, i) for i in range(ends)])  3.84 us
    ppermute x2, waiting for transfers between devices, padded_2(): lax.ppermute(head, axis, [((i + 1) % count, i) for i in range(ends)])  3.19 us
  transfers between devices with their start and end apart: 4, of which 1 were waited for; matrix products, arithmetic and copies ran while one was open for 6% of the time, Pallas kernels for 0%

profile of v1, /device:TPU:1, one launch (start us, length us, event | category | flops | bytes accessed | tf_op | source)
XLA Modules:
  0.0 84.1 jit_solution(1156609977914487084)
XLA Ops:
  0.7 1.2 %fusion.69 = (bf16[1,1,128,640]{3,2,1,0:T(8,128)(2,1)S(1)}, bf16[1,1,128,640]{3,2,1,0:T(8,128)(2,1)S(1)}) fusion(bf16[1,2,128,640]{3,2,1,0:T(8,128)(2,1)} %param.15), kind=kLoop, calls=%fused_computation.109 | loop fusion | bytes 655360 | tf_op jit(solution)/shard_map/slice | solution.py:16
  1.8 4.5 %collective-permute-start.2 = (bf16[1,1,128,640]{3,2,1,0:T(8,128)(2,1)S(1)}, bf16[1,1,128,640]{3,2,1,0:T(8,128)(2,1)S(1)}, u32[]{:S(2)}, u32[]{:S(2)}) collective-permute-start(bf16[1,1,128,640]{3,2,1,0:T(8,128)(2,1)S(1)} %get-tuple-element.30), channel_id=1, source_target_pairs={{0,8},{8,16},{16,24},{1,9},{9,17},{17,25},{2,10},{10,18},{18,26},{... | collective-permute-start | bytes 491528 | tf_op jit(solution)/shard_map/ppermute | solution.py:19
  6.3 1.9 %collective-permute-start.3 = (bf16[1,1,128,640]{3,2,1,0:T(8,128)(2,1)S(1)}, bf16[1,1,128,640]{3,2,1,0:T(8,128)(2,1)S(1)}, u32[]{:S(2)}, u32[]{:S(2)}) collective-permute-start(bf16[1,1,128,640]{3,2,1,0:T(8,128)(2,1)S(1)} %get-tuple-element.31), channel_id=1, source_target_pairs={{8,0},{16,8},{24,16},{9,1},{17,9},{25,17},{10,2},{18,10},{26,18},{... | collective-permute-start | bytes 491528 | tf_op jit(solution)/shard_map/ppermute | solution.py:21
  8.3 1.0 %convert_reduce_fusion.1 = f32[640]{0:T(1024)S(1)} fusion(bf16[1,2,128,640]{3,2,1,0:T(8,128)(2,1)} %param.15), kind=kLoop, calls=%fused_computation.87 | loop fusion | flops 327040 | bytes 330240 | tf_op jit(solution)/shard_map/reduce_sum | solution.py:99
  9.3 1.1 %convert_reduce_fusion = (f32[640]{0:T(1024)S(1)}, f32[640]{0:T(1024)S(1)}) fusion(bf16[1,2,128,640]{3,2,1,0:T(8,128)(2,1)} %param.8), kind=kLoop, calls=%fused_computation.22 | loop fusion | flops 654080 | bytes 332800 | tf_op jit(solution)/shard_map/reduce_sum | solution.py:77
  10.8 5.5 %all-reduce.3 = (f32[1,16]{1,0:T(1,128)S(1)}, f32[1,16]{1,0:T(1,128)S(1)}) all-reduce(f32[1,16]{1,0:T(1,128)S(1)} %bitcast.117, f32[1,16]{1,0:T(1,128)S(1)} %bitcast.116), channel_id=1, replica_groups=mesh['rows'=4,'dp'=8] {'rows'}, use_global_device_ids=true, to_apply=%region_5.6 | all-reduce | flops 32 | bytes 256 | tf_op jit(solution)/shard_map/psum | solution.py:76
  17.9 1.5 %select_maximum_fusion = bf16[1,4,130,640]{3,2,1,0:T(8,128)(2,1)S(1)} fusion(bf16[1,1,128,640]{3,2,1,0:T(8,128)(2,1)S(1)} %collective-permute-done.3, bf16[1,2,128,640]{3,2,1,0:T(8,128)(2,1)} %param.15, bf16[1,1,128,640]{3,2,1,0:T(8,128)(2,1)S(1)} %collective-permute-done.2), kind=kLoop, calls=%fused_computation.63 | loop fusion | flops 3993600 | bytes 1320960 | tf_op jit(solution)/shard_map/concatenate | solution.py:17
  19.6 1.6 %fusion.21 = f32[256,640]{1,0:T(8,128)S(1)} fusion(bf16[256,640]{1,0:T(8,128)(2,1)S(1)} %bitcast.114, bf16[3,3,640,640]{3,2,1,0:T(8,128)(2,1)} %param.12), kind=kOutput, calls=%fused_computation.41 | convolution fusion | flops 209715200 | bytes 1802240 | tf_op jit(solution)/shard_map/dot_general | solution.py:54
  21.3 0.5 fusion.3
  21.8 0.5 convolution_add_fusion.6
  22.3 0.5 convolution_add_fusion.5
  22.8 0.5 convolution_add_fusion.4
  23.3 0.5 convolution_add_fusion.3
  23.8 0.5 convolution_add_fusion.2
  24.2 0.5 convolution_add_fusion.1
  24.7 0.5 fusion.2
  25.7 5.8 %all-reduce.2 = (f32[1,640]{1,0:T(1,128)S(1)}, f32[1,640]{1,0:T(1,128)S(1)}, f32[1,640]{1,0:T(1,128)S(1)}) all-reduce(f32[1,640]{1,0:T(1,128)S(1)} %reduce_sum.117, f32[1,640]{1,0:T(1,128)S(1)} %reduce_sum.120, f32[1,640]{1,0:T(1,128)S(1)} %reduce_sum.123), channel_id=1, replica_groups=mesh['rows'=4,'dp'=8] {'rows'}, use_global_device_ids=true, to_apply=%region_7.8 | all-reduce | flops 1920 | bytes 15360 | tf_op jit(solution)/shard_map/psum | solution.py:100
  31.5 24.7 %all-gather.1 = f32[8,3,640]{2,1,0:T(4,128)S(1)} all-gather(f32[1,3,640]{2,1,0:T(4,128)S(1)} %maximum_bitcast_fusion), channel_id=2, replica_groups=mesh['rows'=4,'dp'=8] {'dp'}, dimensions={0}, use_global_device_ids=true | all-gather | bytes 69120 | tf_op jit(solution)/shard_map/all_gather | solution.py:106
  57.0 10.1 %collective-permute-start = (bf16[1,1,128,640]{3,2,1,0:T(8,128)(2,1)S(1)}, bf16[1,1,128,640]{3,2,1,0:T(8,128)(2,1)S(1)}, u32[]{:S(2)}, u32[]{:S(2)}) collective-permute-start(bf16[1,1,128,640]{3,2,1,0:T(8,128)(2,1)S(1)} %get-tuple-element.34), channel_id=1, source_target_pairs={{0,8},{8,16},{16,24},{1,9},{9,17},{17,25},{2,10},{10,18},{18,26},{... | collective-permute-start | bytes 491528 | tf_op jit(solution)/shard_map/ppermute | solution.py:19
  67.2 1.9 %collective-permute-start.1 = (bf16[1,1,128,640]{3,2,1,0:T(8,128)(2,1)S(1)}, bf16[1,1,128,640]{3,2,1,0:T(8,128)(2,1)S(1)}, u32[]{:S(2)}, u32[]{:S(2)}) collective-permute-start(bf16[1,1,128,640]{3,2,1,0:T(8,128)(2,1)S(1)} %get-tuple-element.35), channel_id=1, source_target_pairs={{8,0},{16,8},{24,16},{9,1},{17,9},{25,17},{10,2},{18,10},{26,18},{... | collective-permute-start | bytes 491528 | tf_op jit(solution)/shard_map/ppermute | solution.py:21
  69.1 0.9 %fusion.61 = bf16[1,2,128,640]{3,2,1,0:T(8,128)(2,1)} fusion(bf16[1,2,128,640]{3,2,1,0:T(8,128)(2,1)S(1)} %copy-done.3, f32[1,2,128,640]{3,2,1,0:T(8,128)S(1)} %get-tuple-element.14, f32[640]{0:T(1024)S(1)} %mul.180, f32[640]{0:T(1024)S(1)} %sub.67, f32[640]{0:T(1024)S(1)} %copy-done.4, f32[640]{0:T(1024)S(1)} %mul.162, f32[640]{0:T(1024)S(1)} %sub.61), kind=kLoop, calls=%fused_computation.85 | loop fusion | flops 1474560 | bytes 1323520 | tf_op jit(solution)/shard_map/convert_element_type | solution.py:113
  70.0 0.6 broadcast_multiply_fusion
  70.6 3.2 %collective-permute-done.1 = bf16[1,1,128,640]{3,2,1,0:T(8,128)(2,1)S(1)} collective-permute-done((bf16[1,1,128,640]{3,2,1,0:T(8,128)(2,1)S(1)}, bf16[1,1,128,640]{3,2,1,0:T(8,128)(2,1)S(1)}, u32[]{:S(2)}, u32[]{:S(2)}) %collective-permute-start.1) | collective-permute-done | bytes 163872 | tf_op jit(solution)/shard_map/ppermute | solution.py:21
  74.3 1.6 %fusion.23 = f32[256,640]{1,0:T(8,128)S(1)} fusion(bf16[256,640]{1,0:T(8,128)(2,1)S(1)} %bitcast.115, bf16[3,3,640,640]{3,2,1,0:T(8,128)(2,1)} %param.12), kind=kOutput, calls=%fused_computation.43 | convolution fusion | flops 209715200 | bytes 1802240 | tf_op jit(solution)/shard_map/dot_general | solution.py:61
  75.9 1.8 %fusion.5 = f32[256,640]{1,0:T(8,128)S(1)} fusion(bf16[256,640]{1,0:T(8,128)(2,1)S(1)} %bitcast.113, bf16[3,3,640,640]{3,2,1,0:T(8,128)(2,1)} %param.12), kind=kOutput, calls=%fused_computation.25 | convolution fusion | flops 209715200 | bytes 1802240 | tf_op jit(solution)/shard_map/dot_general | solution.py:61
  77.7 1.6 %convolution_add_fusion.13 = f32[256,640]{1,0:T(8,128)S(1)} fusion(f32[256,640]{1,0:T(8,128)S(1)} %fusion.23, bf16[256,640]{1,0:T(8,128)(2,1)S(1)} %bitcast.103, bf16[3,3,640,640]{3,2,1,0:T(8,128)(2,1)} %param.12), kind=kOutput, calls=%fused_computation.16 | convolution fusion | flops 209879040 | bytes 2457600 | tf_op jit(solution)/shard_map/dot_general | solution.py:61
  79.4 1.6 %convolution_add_fusion.12 = f32[256,640]{1,0:T(8,128)S(1)} fusion(f32[256,640]{1,0:T(8,128)S(1)} %convolution_add_fusion.13, bf16[256,640]{1,0:T(8,128)(2,1)S(1)} %bitcast.111, bf16[3,3,640,640]{3,2,1,0:T(8,128)(2,1)} %param.12), kind=kOutput, calls=%fused_computation.15 | convolution fusion | flops 209879040 | bytes 2457600 | tf_op jit(solution)/shard_map/dot_general | solution.py:61
  81.5 0.5 convolution_add_fusion.10
  81.9 0.5 convolution_add_fusion.9
  82.4 0.5 convolution_add_fusion.8
  82.9 0.5 fusion.1
  83.4 0.8 add_convert_fusion
  (59 shorter events, 3.7 us)
Async XLA Ops:
  0.6 16.9 %copy-start = (bf16[1280,640]{1,0:T(8,128)(2,1)S(1)}, bf16[1280,640]{1,0:T(8,128)(2,1)}, u32[]{:S(2)}) copy-start(bf16[1280,640]{1,0:T(8,128)(2,1)} %param.14) | copy-start | bytes 4915204
  0.6 21.1 %copy-start.2 = (bf16[1,2,128,640]{3,2,1,0:T(8,128)(2,1)S(1)}, bf16[1,2,128,640]{3,2,1,0:T(8,128)(2,1)}, u32[]{:S(2)}) copy-start(bf16[1,2,128,640]{3,2,1,0:T(8,128)(2,1)} %param.15) | copy-start | bytes 983044
  1.8 16.1 %collective-permute-start.2 = (bf16[1,1,128,640]{3,2,1,0:T(8,128)(2,1)S(1)}, bf16[1,1,128,640]{3,2,1,0:T(8,128)(2,1)S(1)}, u32[]{:S(2)}, u32[]{:S(2)}) collective-permute-start(bf16[1,1,128,640]{3,2,1,0:T(8,128)(2,1)S(1)} %get-tuple-element.30), channel_id=1, source_target_pairs={{0,8},{8,16},{16,24},{1,9},{9,17},{17,25},{2,10},{10,18},{18,26},{... | collective-permute-start | bytes 491528 | tf_op jit(solution)/shard_map/ppermute | solution.py:19
  6.3 11.6 %collective-permute-start.3 = (bf16[1,1,128,640]{3,2,1,0:T(8,128)(2,1)S(1)}, bf16[1,1,128,640]{3,2,1,0:T(8,128)(2,1)S(1)}, u32[]{:S(2)}, u32[]{:S(2)}) collective-permute-start(bf16[1,1,128,640]{3,2,1,0:T(8,128)(2,1)S(1)} %get-tuple-element.31), channel_id=1, source_target_pairs={{8,0},{16,8},{24,16},{9,1},{17,9},{25,17},{10,2},{18,10},{26,18},{... | collective-permute-start | bytes 491528 | tf_op jit(solution)/shard_map/ppermute | solution.py:21
  16.6 4.6 %copy-start.1 = (bf16[3,3,640,640]{3,2,1,0:T(8,128)(2,1)S(1)}, bf16[3,3,640,640]{3,2,1,0:T(8,128)(2,1)}, u32[]{:S(2)}) copy-start(bf16[3,3,640,640]{3,2,1,0:T(8,128)(2,1)} %param.12) | copy-start | bytes 22118404
  22.3 2.9 %copy-start.3 = (bf16[1,2,128,640]{3,2,1,0:T(8,128)(2,1)S(1)}, bf16[1,2,128,640]{3,2,1,0:T(8,128)(2,1)}, u32[]{:S(2)}) copy-start(bf16[1,2,128,640]{3,2,1,0:T(8,128)(2,1)} %param.8) | copy-start | bytes 983044
  22.3 2.9 %copy-start.4 = (f32[640]{0:T(1024)S(1)}, f32[640]{0:T(1024)}, u32[]{:S(2)}) copy-start(f32[640]{0:T(1024)} %param.10) | copy-start | bytes 7684
  22.3 2.9 %copy-start.5 = (f32[640]{0:T(1024)S(1)}, f32[640]{0:T(1024)}, u32[]{:S(2)}) copy-start(f32[640]{0:T(1024)} %param.11) | copy-start | bytes 7684
  57.0 13.6 %collective-permute-start = (bf16[1,1,128,640]{3,2,1,0:T(8,128)(2,1)S(1)}, bf16[1,1,128,640]{3,2,1,0:T(8,128)(2,1)S(1)}, u32[]{:S(2)}, u32[]{:S(2)}) collective-permute-start(bf16[1,1,128,640]{3,2,1,0:T(8,128)(2,1)S(1)} %get-tuple-element.34), channel_id=1, source_target_pairs={{0,8},{8,16},{16,24},{1,9},{9,17},{17,25},{2,10},{10,18},{18,26},{... | collective-permute-start | bytes 491528 | tf_op jit(solution)/shard_map/ppermute | solution.py:19
  67.2 6.6 %collective-permute-start.1 = (bf16[1,1,128,640]{3,2,1,0:T(8,128)(2,1)S(1)}, bf16[1,1,128,640]{3,2,1,0:T(8,128)(2,1)S(1)}, u32[]{:S(2)}, u32[]{:S(2)}) collective-permute-start(bf16[1,1,128,640]{3,2,1,0:T(8,128)(2,1)S(1)} %get-tuple-element.35), channel_id=1, source_target_pairs={{8,0},{16,8},{24,16},{9,1},{17,9},{25,17},{10,2},{18,10},{26,18},{... | collective-permute-start | bytes 491528 | tf_op jit(solution)/shard_map/ppermute | solution.py:21
  70.6 10.4 %slice-start = ((s8[7372800]{0:T(1024)(128)(4,1)}), s8[3178496]{0:T(1024)(128)(4,1)S(1)}, s32[]{:S(2)}) async-start(s8[7372800]{0:T(1024)(128)(4,1)} %bitcast.95), calls=%async_computation | async-start | bytes 6356992
  75.9 5.1 %slice-start.1 = ((s8[7372800]{0:T(1024)(128)(4,1)}), s8[4194304]{0:T(1024)(128)(4,1)S(1)}, s32[]{:S(2)}) async-start(s8[7372800]{0:T(1024)(128)(4,1)} %bitcast.95), calls=%async_computation.1 | async-start | bytes 8388608
  79.4 4.0 %copy-start.6 = (f32[640]{0:T(1024)S(1)}, f32[640]{0:T(1024)}, u32[]{:S(2)}) copy-start(f32[640]{0:T(1024)} %param.13) | copy-start | bytes 7684
